TPU v7x, 32 devices: a whole 2x2x4 slice. The times are simulated.
32 devices in a mesh: blk: 16 (over z, y, core), rhs: 2 (over x).
Axes of the slice: x: 2, y: 2, z: 4, core: 2. Of those that a mesh axis runs over, the one named last changes fastest.
Arguments:
- factor_panel: float32 [2, 1024, 16384], P(None, None, 'blk'), may hold values from -0.0625 to 0.0625
- solved_before: float32 [16384, 512], P('blk', 'rhs'), may hold values from -6 to 6
- right_side: float32 [2, 1024, 512], P(None, None, 'rhs'), may hold values from -6 to 6
- diag_inverse: float32 [2, 1024, 1024], P(None, 'blk', 'rhs'), may hold values from -0.2 to 1.5, as said below
- coupling: float32 [1024, 1024], P(None, 'blk'), may hold values from -0.25 to 0.25
Outputs:
- solved: float32 [2, 1024, 512], P(None, 'blk', 'rhs')
Inputs may be any that keep to these rules, and one draw needn't show every extreme that they name: `diag_inverse`: each of the two blocks is lower triangular with a positive diagonal.
All inputs are finite; a program needn't handle non-finite values.
Results may differ from a plain program's by a relative error of at most 0.00009.
Values sent between devices are 32-bit elements; how exact they have to be, the bound alone decides.
No kernel may reach another device: no remote copies, remote signals or barrier semaphores. Data moves between devices by JAX's collectives and lax.ppermute only.
A program may use at most 64 MiB of HBM per device.

v0:
```python
import jax
import jax.numpy as jnp
from jax import lax
from jax.sharding import PartitionSpec as P


def product(left, right):
    return jnp.dot(left, right, precision=lax.Precision.HIGHEST, preferred_element_type=jnp.float32)


def shards(factor_panel, solved_before, right_side, diag_inverse, coupling):
    inverse_full = lax.all_gather(diag_inverse, "rhs", axis=2, tiled=True)
    own_count = diag_inverse.shape[1]
    my_index = lax.axis_index("blk")

    def own_slice(matrix):
        return lax.dynamic_slice_in_dim(matrix, my_index * own_count, own_count, 0)

    first_part = lax.psum_scatter(
        product(factor_panel[0], solved_before), "blk", scatter_dimension=0, tiled=True
    )
    first_remains = lax.all_gather(own_slice(right_side[0]) - first_part, "blk", axis=0, tiled=True)
    first_block = product(inverse_full[0], first_remains)
    panel_rows = factor_panel[1]
    second_part = lax.psum_scatter(
        product(panel_rows, solved_before) + product(coupling, first_block),
        "blk",
        scatter_dimension=0,
        tiled=True,
    )
    second_remains = lax.all_gather(
        own_slice(right_side[1]) - second_part, "blk", axis=0, tiled=True
    )
    second_block = product(inverse_full[1], second_remains)
    return jnp.stack([first_block, second_block])


def solution(mesh):
    placed = (
        P(None, None, "blk"),
        P("blk", "rhs"),
        P(None, None, "rhs"),
        P(None, "blk", "rhs"),
        P(None, "blk"),
    )
    return jax.shard_map(
        shards, mesh=mesh, in_specs=placed, out_specs=P(None, "blk", "rhs"), check_vma=False
    )
```

profile of v0, /device:TPU:0, one launch (start us, length us, event | category | flops | bytes accessed | tf_op | source)
XLA Modules:
  0.0 229.3 jit_solution(9284285652021798626)
XLA Ops:
  6.5 0.0 copy-start
  6.5 1.2 copy-done
  7.8 6.6 %fusion.2 = f32[1024,256]{1,0:T(8,128)} fusion(f32[1024,256]{1,0:T(8,128)S(1)} %copy-done, f32[2,1024,1024]{2,1,0:T(8,128)} %param.5), kind=kOutput, calls=%fused_computation.2 | convolution fusion | flops 3221225472 | bytes 6291456 | tf_op jit(solution)/shard_map/dot_general | solution.py:8
  14.4 0.0 reduce-scatter.3.cloned.1.call-update
  14.4 0.0 all-gather.3.cloned.1.call-start
  14.5 0.0 copy-done.1
  14.5 1.5 fusion.10
  16.0 58.7 %reduce-scatter.3.cloned.1.call-done = f32[64,256]{1,0:T(8,128)} async-done(((f32[1024,256]{1,0:T(8,128)}), f32[64,256]{1,0:T(8,128)}) %reduce-scatter.3.cloned.1.call-update) | async-done | bytes 65552 | tf_op jit(solution)/shard_map/reduce_scatter | solution.py:19
  74.7 1.5 bitcast_subtract_fusion.1
  76.2 0.0 all-gather.3.cloned.1.call-update
  76.2 0.0 reduce-scatter.5.cloned.1.call-start
  76.3 7.0 %all_gather.10 = f32[2,64,1024]{2,1,0:T(8,128)S(1)} all-gather(f32[2,64,512]{2,1,0:T(8,128)S(1)} %copy-done.2), channel_id=1, replica_groups=mesh['blk'=16,'rhs'=2] {'rhs'}, dimensions={2}, use_global_device_ids=true | all-gather | bytes 786432 | tf_op jit(solution)/shard_map/all_gather | solution.py:12
  83.3 30.7 %all-gather.3.cloned.1.call-done = f32[1024,256]{1,0:T(8,128)} async-done(((f32[64,256]{1,0:T(8,128)}), f32[1024,256]{1,0:T(8,128)}) %all-gather.3.cloned.1.call-update) | async-done | bytes 1048592 | tf_op jit(solution)/shard_map/all_gather | solution.py:22
  114.0 2.0 fusion.9
  116.0 2.0 convolution_bitcast_fusion
  118.0 6.6 %fusion.6 = f32[1024,256]{1,0:T(8,128)} fusion(f32[1024,256]{1,0:T(8,128)S(1)} %convolution_bitcast_fusion, f32[1024,256]{1,0:T(8,128)S(1)} %copy-done, f32[2,1024,1024]{2,1,0:T(8,128)} %param.5), kind=kOutput, calls=%fused_computation.6 | convolution fusion | flops 3221487616 | bytes 7340032 | tf_op jit(solution)/shard_map/dot_general | solution.py:8
  124.6 0.0 reduce-scatter.5.cloned.1.call-update
  124.6 0.0 all-gather.5.cloned.1.call-start
  124.7 56.4 %reduce-scatter.5.cloned.1.call-done = f32[64,256]{1,0:T(8,128)} async-done(((f32[1024,256]{1,0:T(8,128)}), f32[64,256]{1,0:T(8,128)}) %reduce-scatter.5.cloned.1.call-update) | async-done | bytes 65552 | tf_op jit(solution)/shard_map/reduce_scatter | solution.py:25
  181.1 1.5 bitcast_subtract_fusion
  182.6 0.0 all-gather.5.cloned.1.call-update
  182.6 37.5 %all-gather.5.cloned.1.call-done = f32[1024,256]{1,0:T(8,128)} async-done(((f32[64,256]{1,0:T(8,128)}), f32[1024,256]{1,0:T(8,128)}) %all-gather.5.cloned.1.call-update) | async-done | bytes 1048592 | tf_op jit(solution)/shard_map/all_gather | solution.py:31
  220.1 2.0 convolution_bitcast_fusion.1
  222.1 0.7 pad_maximum_fusion
  (4 shorter events, 0.0 us)
Async XLA Ops:
  6.5 1.2 copy-start
  6.5 7.9 %copy-start.1 = (f32[2,1024,256]{2,1,0:T(8,128)S(1)}, f32[2,1024,256]{2,1,0:T(8,128)}, u32[]{:S(2)}) copy-start(f32[2,1024,256]{2,1,0:T(8,128)} %param.7) | copy-start | bytes 6291460
  6.5 68.2 %reduce-scatter.3.cloned.1.call-start = ((), (), s32[]{:S(2)}) async-start(), calls=%async_computation.2 | async-start | bytes 1114112 | tf_op jit(solution)/shard_map/reduce_scatter | solution.py:19
  14.4 61.9 %copy-start.2 = (f32[2,64,512]{2,1,0:T(8,128)S(1)}, f32[2,64,512]{2,1,0:T(8,128)}, u32[]{:S(2)}) copy-start(f32[2,64,512]{2,1,0:T(8,128)} %param.8) | copy-start | bytes 786436
  14.4 99.6 %all-gather.3.cloned.1.call-start = ((), (), s32[]{:S(2)}) async-start(), calls=%async_computation.3 | async-start | bytes 1114112 | tf_op jit(solution)/shard_map/all_gather | solution.py:22
  76.2 104.9 %reduce-scatter.5.cloned.1.call-start = ((), (), s32[]{:S(2)}) async-start(), calls=%async_computation.4 | async-start | bytes 1114112 | tf_op jit(solution)/shard_map/reduce_scatter | solution.py:25
  124.6 95.5 %all-gather.5.cloned.1.call-start = ((), (), s32[]{:S(2)}) async-start(), calls=%async_computation.5 | async-start | bytes 1114112 | tf_op jit(solution)/shard_map/all_gather | solution.py:31
Sparse Core Ops, SparseCore 0:
  14.5 60.1 reduce-scatter.2
  77.1 36.8 all-gather.2
  124.7 56.3 reduce-scatter.4
  183.1 36.9 all-gather.4
where the time goes:
time: 230 us; the launch traced here: 229 us
  waiting for transfers between devices  183 us (80%)
  matrix products  19.1 us (8%)
  between operations  13.2 us (6%)
  blocking collectives  7.05 us (3%)
  other arithmetic  3.69 us (2%)
  local copies, waits for them, and re-layouts  2.72 us (1%)
    reduce_scatter x1, waiting for transfers between devices, shards(): lax.psum_scatter(product(factor_panel[0], solved_before), 'blk', scatter_...  58.7 us
    reduce_scatter x1, waiting for transfers between devices, shards(): lax.psum_scatter(product(panel_rows, solved_before) + product(coupling, f...  56.4 us
    all_gather x1, waiting for transfers between devices, shards(): lax.all_gather(own_slice(right_side[1]) - second_part, 'blk', axis=0, til...  37.5 us
    all_gather x1, waiting for transfers between devices, shards(): lax.all_gather(own_slice(right_side[0]) - first_part, 'blk', axis=0, tile...  30.7 us
    dot_general x5, matrix products, product(): jnp.dot(left, right, precision=lax.Precision.HIGHEST, preferred_element_t...  19.1 us
    all_gather x1, blocking collectives, shards(): inverse_full = lax.all_gather(diag_inverse, 'rhs', axis=2, tiled=True)  7.05 us
  transfers between devices with their start and end apart: 4, of which 4 were waited for; matrix products, arithmetic and copies ran while one was open for 1% of the time, Pallas kernels for 0%

commit v1 on v0

--- a/solution.py
+++ b/solution.py
@@ -9,6 +9,26 @@
 
 
 def shards(factor_panel, solved_before, right_side, diag_inverse, coupling):
+
+    def group_the_tails(vals, peer_axis):
+        trail = []
+        full_n = jax.lax.axis_size(peer_axis)
+        for idx in range(full_n):
+            trail.append((idx, (idx + 1) % full_n))
+        sides = []
+        for idx in range(full_n):
+            sides.append((idx, (idx - 1) % full_n))
+        f_next, q_next = ([vals], [vals])
+        for _ in range(full_n // 2):
+            f_next.append(jax.lax.ppermute(f_next[-1], peer_axis, trail))
+        for _ in range((full_n - 1) // 2):
+            q_next.append(jax.lax.ppermute(q_next[-1], peer_axis, perm=sides))
+        return jnp.roll(
+            jnp.concatenate([*f_next[::-1], *q_next[1:]], 0),
+            (jax.lax.axis_index(peer_axis) - full_n // 2) * vals.shape[0],
+            axis=0,
+        )
+
     inverse_full = lax.all_gather(diag_inverse, "rhs", axis=2, tiled=True)
     own_count = diag_inverse.shape[1]
     my_index = lax.axis_index("blk")
@@ -28,9 +48,7 @@
         scatter_dimension=0,
         tiled=True,
     )
-    second_remains = lax.all_gather(
-        own_slice(right_side[1]) - second_part, "blk", axis=0, tiled=True
-    )
+    second_remains = group_the_tails(own_slice(right_side[1]) - second_part, "blk")
     second_block = product(inverse_full[1], second_remains)
     return jnp.stack([first_block, second_block])
 

time: 230 us -> 241 us (1.048)
  starting transfers between devices: 0.13 us -> 31.5 us
  waiting for transfers between devices: 183 us -> 166 us
    all_gather x1 -> x0, waiting for transfers between devices: 37.5 us -> none  [shards(): lax.all_gather(own_slice(right_side[1]) - second_part, 'blk', axis=0, til...]
    ppermute x0 -> x15, starting transfers between devices: none -> 31.4 us  [the longest x7 31.3 us: group_the_tails(): q_next.append(jax.lax.ppermute(q_next[-1], peer_axis, perm=sides))]
    ppermute x0 -> x15, waiting for transfers between devices: none -> 19.9 us  [the longest x8 19.8 us: group_the_tails(): f_next.append(jax.lax.ppermute(f_next[-1], peer_axis, trail))]
  transfers between devices with their start and end apart: 4 -> 18, of which waited for: 4 -> 11; matrix products, arithmetic and copies ran while one was open for 1% -> 1% of each run, Pallas kernels for 0% -> 0%
where the time goes in v1:
time: 241 us
  waiting for transfers between devices  166 us (69%)
  starting transfers between devices  31.5 us (13%)
  matrix products  17 us (7%)
  between operations  13.4 us (6%)
  blocking collectives  7.05 us (3%)
  other arithmetic  3.06 us (1%)
  local copies, waits for them, and re-layouts  2.91 us (1%)
    reduce_scatter x1, waiting for transfers between devices, shards(): lax.psum_scatter(product(factor_panel[0], solved_before), 'blk', scatter_...  58.7 us
    reduce_scatter x1, waiting for transfers between devices, shards(): lax.psum_scatter(product(panel_rows, solved_before) + product(coupling, f...  56.5 us
    ppermute x7, starting transfers between devices, group_the_tails(): q_next.append(jax.lax.ppermute(q_next[-1], peer_axis, perm=sides))  31.3 us
    all_gather x1, waiting for transfers between devices, shards(): lax.all_gather(own_slice(right_side[0]) - first_part, 'blk', axis=0, tile...  30.7 us
    ppermute x8, waiting for transfers between devices, group_the_tails(): f_next.append(jax.lax.ppermute(f_next[-1], peer_axis, trail))  19.8 us
    dot_general x5, matrix products, product(): jnp.dot(left, right, precision=lax.Precision.HIGHEST, preferred_element_t...  17 us
    all_gather x1, blocking collectives, shards(): inverse_full = lax.all_gather(diag_inverse, 'rhs', axis=2, tiled=True)  7.05 us
  transfers between devices with their start and end apart: 18, of which 11 were waited for; matrix products, arithmetic and copies ran while one was open for 1% of the time, Pallas kernels for 0%

profile of v1, /device:TPU:0, one launch (start us, length us, event | category | flops | bytes accessed | tf_op | source)
XLA Modules:
  0.0 240.8 jit_solution(12434817027093254538)
XLA Ops:
  7.8 6.7 %fusion.2 = f32[1024,256]{1,0:T(8,128)} fusion(f32[1024,256]{1,0:T(8,128)S(1)} %copy-done, f32[2,1024,1024]{2,1,0:T(8,128)} %param.5), kind=kOutput, calls=%fused_computation.2 | convolution fusion | flops 3221225472 | bytes 6291456 | tf_op jit(solution)/shard_map/dot_general | solution.py:8
  14.6 1.5 fusion.12
  16.0 58.7 %reduce-scatter.3.cloned.1.call-done = f32[64,256]{1,0:T(8,128)} async-done(((f32[1024,256]{1,0:T(8,128)}), f32[64,256]{1,0:T(8,128)}) %reduce-scatter.3.cloned.1.call-update) | async-done | bytes 65552 | tf_op jit(solution)/shard_map/reduce_scatter | solution.py:39
  74.8 1.5 bitcast_subtract_fusion.1
  76.4 7.0 %all_gather.7 = f32[2,64,1024]{2,1,0:T(8,128)S(1)} all-gather(f32[2,64,512]{2,1,0:T(8,128)S(1)} %copy-done.2), channel_id=1, replica_groups=mesh['blk'=16,'rhs'=2] {'rhs'}, dimensions={2}, use_global_device_ids=true | all-gather | bytes 786432 | tf_op jit(solution)/shard_map/all_gather | solution.py:32
  83.4 30.7 %all-gather.2.cloned.1.call-done = f32[1024,256]{1,0:T(8,128)} async-done(((f32[64,256]{1,0:T(8,128)}), f32[1024,256]{1,0:T(8,128)}) %all-gather.2.cloned.1.call-update) | async-done | bytes 1048592 | tf_op jit(solution)/shard_map/all_gather | solution.py:42
  114.1 2.0 fusion.10
  117.1 6.6 %fusion.6 = f32[1024,256]{1,0:T(8,128)} fusion(f32[1024,256]{1,0:T(8,128)S(1)} %convolution_bitcast_fusion, f32[1024,256]{1,0:T(8,128)S(1)} %copy-done, f32[2,1024,1024]{2,1,0:T(8,128)} %param.5), kind=kOutput, calls=%fused_computation.6 | convolution fusion | flops 3221487616 | bytes 7340032 | tf_op jit(solution)/shard_map/dot_general | solution.py:8
  123.7 56.5 %reduce-scatter.5.cloned.1.call-done = f32[64,256]{1,0:T(8,128)} async-done(((f32[1024,256]{1,0:T(8,128)}), f32[64,256]{1,0:T(8,128)}) %reduce-scatter.5.cloned.1.call-update) | async-done | bytes 65552 | tf_op jit(solution)/shard_map/reduce_scatter | solution.py:45
  181.2 6.4 %collective-permute-done = f32[64,256]{1,0:T(8,128)S(1)} collective-permute-done((f32[64,256]{1,0:T(8,128)S(1)}, f32[64,256]{1,0:T(8,128)S(1)}, u32[]{:S(2)}, u32[]{:S(2)}) %collective-permute-start) | collective-permute-done | bytes 65568 | tf_op jit(solution)/shard_map/ppermute | solution.py:23
  187.6 4.4 %collective-permute-start.8 = (f32[64,256]{1,0:T(8,128)S(1)}, f32[64,256]{1,0:T(8,128)S(1)}, u32[]{:S(2)}, u32[]{:S(2)}) collective-permute-start(f32[64,256]{1,0:T(8,128)S(1)} %bitcast_subtract_fusion), channel_id=1, source_target_pairs={{0,30},{2,0},{4,2},{6,4},{8,6},{10,8},{12,10},{14,12},{16,14},{18,... | collective-permute-start | bytes 196616 | tf_op jit(solution)/shard_map/ppermute | solution.py:25
  192.0 2.0 collective-permute-done.1
  194.1 4.4 %collective-permute-start.9 = (f32[64,256]{1,0:T(8,128)S(1)}, f32[64,256]{1,0:T(8,128)S(1)}, u32[]{:S(2)}, u32[]{:S(2)}) collective-permute-start(f32[64,256]{1,0:T(8,128)S(1)} %collective-permute-done.8), channel_id=1, source_target_pairs={{0,30},{2,0},{4,2},{6,4},{8,6},{10,8},{12,10},{14,12},{16,14},{18,... | collective-permute-start | bytes 196616 | tf_op jit(solution)/shard_map/ppermute | solution.py:25
  198.5 1.9 collective-permute-done.2
  200.4 4.5 %collective-permute-start.10 = (f32[64,256]{1,0:T(8,128)S(1)}, f32[64,256]{1,0:T(8,128)S(1)}, u32[]{:S(2)}, u32[]{:S(2)}) collective-permute-start(f32[64,256]{1,0:T(8,128)S(1)} %collective-permute-done.9), channel_id=1, source_target_pairs={{0,30},{2,0},{4,2},{6,4},{8,6},{10,8},{12,10},{14,12},{16,14},{18,... | collective-permute-start | bytes 196616 | tf_op jit(solution)/shard_map/ppermute | solution.py:25
  204.9 1.9 collective-permute-done.3
  206.9 4.5 %collective-permute-start.11 = (f32[64,256]{1,0:T(8,128)S(1)}, f32[64,256]{1,0:T(8,128)S(1)}, u32[]{:S(2)}, u32[]{:S(2)}) collective-permute-start(f32[64,256]{1,0:T(8,128)S(1)} %collective-permute-done.10), channel_id=1, source_target_pairs={{0,30},{2,0},{4,2},{6,4},{8,6},{10,8},{12,10},{14,12},{16,14},{18,... | collective-permute-start | bytes 196616 | tf_op jit(solution)/shard_map/ppermute | solution.py:25
  211.3 1.9 collective-permute-done.4
  213.2 4.5 %collective-permute-start.12 = (f32[64,256]{1,0:T(8,128)S(1)}, f32[64,256]{1,0:T(8,128)S(1)}, u32[]{:S(2)}, u32[]{:S(2)}) collective-permute-start(f32[64,256]{1,0:T(8,128)S(1)} %collective-permute-done.11), channel_id=1, source_target_pairs={{0,30},{2,0},{4,2},{6,4},{8,6},{10,8},{12,10},{14,12},{16,14},{18,... | collective-permute-start | bytes 196616 | tf_op jit(solution)/shard_map/ppermute | solution.py:25
  217.7 1.9 collective-permute-done.5
  219.6 4.5 %collective-permute-start.13 = (f32[64,256]{1,0:T(8,128)S(1)}, f32[64,256]{1,0:T(8,128)S(1)}, u32[]{:S(2)}, u32[]{:S(2)}) collective-permute-start(f32[64,256]{1,0:T(8,128)S(1)} %collective-permute-done.12), channel_id=1, source_target_pairs={{0,30},{2,0},{4,2},{6,4},{8,6},{10,8},{12,10},{14,12},{16,14},{18,... | collective-permute-start | bytes 196616 | tf_op jit(solution)/shard_map/ppermute | solution.py:25
  224.1 1.9 collective-permute-done.6
  226.0 4.5 %collective-permute-start.14 = (f32[64,256]{1,0:T(8,128)S(1)}, f32[64,256]{1,0:T(8,128)S(1)}, u32[]{:S(2)}, u32[]{:S(2)}) collective-permute-start(f32[64,256]{1,0:T(8,128)S(1)} %collective-permute-done.13), channel_id=1, source_target_pairs={{0,30},{2,0},{4,2},{6,4},{8,6},{10,8},{12,10},{14,12},{16,14},{18,... | collective-permute-start | bytes 196616 | tf_op jit(solution)/shard_map/ppermute | solution.py:25
  230.5 1.9 collective-permute-done.7
  (65 shorter events, 5.1 us)
Async XLA Ops:
  6.5 1.2 copy-start
  6.5 68.2 %reduce-scatter.3.cloned.1.call-start = ((), (), s32[]{:S(2)}) async-start(), calls=%async_computation.2 | async-start | bytes 1114112 | tf_op jit(solution)/shard_map/reduce_scatter | solution.py:39
  7.8 6.8 %copy-start.1 = (f32[2,1024,256]{2,1,0:T(8,128)S(1)}, f32[2,1024,256]{2,1,0:T(8,128)}, u32[]{:S(2)}) copy-start(f32[2,1024,256]{2,1,0:T(8,128)} %param.7) | copy-start | bytes 6291460
  14.5 99.6 %all-gather.2.cloned.1.call-start = ((), (), s32[]{:S(2)}) async-start(), calls=%async_computation.3 | async-start | bytes 1114112 | tf_op jit(solution)/shard_map/all_gather | solution.py:42
  14.6 61.8 %copy-start.2 = (f32[2,64,512]{2,1,0:T(8,128)S(1)}, f32[2,64,512]{2,1,0:T(8,128)}, u32[]{:S(2)}) copy-start(f32[2,64,512]{2,1,0:T(8,128)} %param.8) | copy-start | bytes 786436
  16.0 100.0 %copy-start.3 = (f32[1024,64]{0,1:T(8,128)S(1)}, f32[1024,64]{0,1:T(8,128)}, u32[]{:S(2)}) copy-start(f32[1024,64]{0,1:T(8,128)} %param.9) | copy-start | bytes 786436
  76.3 103.9 %reduce-scatter.5.cloned.1.call-start = ((), (), s32[]{:S(2)}) async-start(), calls=%async_computation.4 | async-start | bytes 1114112 | tf_op jit(solution)/shard_map/reduce_scatter | solution.py:45
  181.1 6.4 %collective-permute-start = (f32[64,256]{1,0:T(8,128)S(1)}, f32[64,256]{1,0:T(8,128)S(1)}, u32[]{:S(2)}, u32[]{:S(2)}) collective-permute-start(f32[64,256]{1,0:T(8,128)S(1)} %bitcast_subtract_fusion), channel_id=1, source_target_pairs={{0,2},{2,4},{4,6},{6,8},{8,10},{10,12},{12,14},{14,16},{16,18},{18... | collective-permute-start | bytes 196616 | tf_op jit(solution)/shard_map/ppermute | solution.py:23
  187.6 6.5 %collective-permute-start.1 = (f32[64,256]{1,0:T(8,128)S(1)}, f32[64,256]{1,0:T(8,128)S(1)}, u32[]{:S(2)}, u32[]{:S(2)}) collective-permute-start(f32[64,256]{1,0:T(8,128)S(1)} %collective-permute-done), channel_id=1, source_target_pairs={{0,2},{2,4},{4,6},{6,8},{8,10},{10,12},{12,14},{14,16},{16,18},{18... | collective-permute-start | bytes 196616 | tf_op jit(solution)/shard_map/ppermute | solution.py:23
  187.6 6.5 %collective-permute-start.8 = (f32[64,256]{1,0:T(8,128)S(1)}, f32[64,256]{1,0:T(8,128)S(1)}, u32[]{:S(2)}, u32[]{:S(2)}) collective-permute-start(f32[64,256]{1,0:T(8,128)S(1)} %bitcast_subtract_fusion), channel_id=1, source_target_pairs={{0,30},{2,0},{4,2},{6,4},{8,6},{10,8},{12,10},{14,12},{16,14},{18,... | collective-permute-start | bytes 196616 | tf_op jit(solution)/shard_map/ppermute | solution.py:25
  194.1 6.4 %collective-permute-start.2 = (f32[64,256]{1,0:T(8,128)S(1)}, f32[64,256]{1,0:T(8,128)S(1)}, u32[]{:S(2)}, u32[]{:S(2)}) collective-permute-start(f32[64,256]{1,0:T(8,128)S(1)} %collective-permute-done.1), channel_id=1, source_target_pairs={{0,2},{2,4},{4,6},{6,8},{8,10},{10,12},{12,14},{14,16},{16,18},{18... | collective-permute-start | bytes 196616 | tf_op jit(solution)/shard_map/ppermute | solution.py:23
  194.1 6.4 %collective-permute-start.9 = (f32[64,256]{1,0:T(8,128)S(1)}, f32[64,256]{1,0:T(8,128)S(1)}, u32[]{:S(2)}, u32[]{:S(2)}) collective-permute-start(f32[64,256]{1,0:T(8,128)S(1)} %collective-permute-done.8), channel_id=1, source_target_pairs={{0,30},{2,0},{4,2},{6,4},{8,6},{10,8},{12,10},{14,12},{16,14},{18,... | collective-permute-start | bytes 196616 | tf_op jit(solution)/shard_map/ppermute | solution.py:25
  200.4 6.4 %collective-permute-start.3 = (f32[64,256]{1,0:T(8,128)S(1)}, f32[64,256]{1,0:T(8,128)S(1)}, u32[]{:S(2)}, u32[]{:S(2)}) collective-permute-start(f32[64,256]{1,0:T(8,128)S(1)} %collective-permute-done.2), channel_id=1, source_target_pairs={{0,2},{2,4},{4,6},{6,8},{8,10},{10,12},{12,14},{14,16},{16,18},{18... | collective-permute-start | bytes 196616 | tf_op jit(solution)/shard_map/ppermute | solution.py:23
  200.4 6.4 %collective-permute-start.10 = (f32[64,256]{1,0:T(8,128)S(1)}, f32[64,256]{1,0:T(8,128)S(1)}, u32[]{:S(2)}, u32[]{:S(2)}) collective-permute-start(f32[64,256]{1,0:T(8,128)S(1)} %collective-permute-done.9), channel_id=1, source_target_pairs={{0,30},{2,0},{4,2},{6,4},{8,6},{10,8},{12,10},{14,12},{16,14},{18,... | collective-permute-start | bytes 196616 | tf_op jit(solution)/shard_map/ppermute | solution.py:25
  206.8 6.4 %collective-permute-start.4 = (f32[64,256]{1,0:T(8,128)S(1)}, f32[64,256]{1,0:T(8,128)S(1)}, u32[]{:S(2)}, u32[]{:S(2)}) collective-permute-start(f32[64,256]{1,0:T(8,128)S(1)} %collective-permute-done.3), channel_id=1, source_target_pairs={{0,2},{2,4},{4,6},{6,8},{8,10},{10,12},{12,14},{14,16},{16,18},{18... | collective-permute-start | bytes 196616 | tf_op jit(solution)/shard_map/ppermute | solution.py:23
  206.9 6.4 %collective-permute-start.11 = (f32[64,256]{1,0:T(8,128)S(1)}, f32[64,256]{1,0:T(8,128)S(1)}, u32[]{:S(2)}, u32[]{:S(2)}) collective-permute-start(f32[64,256]{1,0:T(8,128)S(1)} %collective-permute-done.10), channel_id=1, source_target_pairs={{0,30},{2,0},{4,2},{6,4},{8,6},{10,8},{12,10},{14,12},{16,14},{18,... | collective-permute-start | bytes 196616 | tf_op jit(solution)/shard_map/ppermute | solution.py:25
  213.2 6.4 %collective-permute-start.5 = (f32[64,256]{1,0:T(8,128)S(1)}, f32[64,256]{1,0:T(8,128)S(1)}, u32[]{:S(2)}, u32[]{:S(2)}) collective-permute-start(f32[64,256]{1,0:T(8,128)S(1)} %collective-permute-done.4), channel_id=1, source_target_pairs={{0,2},{2,4},{4,6},{6,8},{8,10},{10,12},{12,14},{14,16},{16,18},{18... | collective-permute-start | bytes 196616 | tf_op jit(solution)/shard_map/ppermute | solution.py:23
  213.2 6.4 %collective-permute-start.12 = (f32[64,256]{1,0:T(8,128)S(1)}, f32[64,256]{1,0:T(8,128)S(1)}, u32[]{:S(2)}, u32[]{:S(2)}) collective-permute-start(f32[64,256]{1,0:T(8,128)S(1)} %collective-permute-done.11), channel_id=1, source_target_pairs={{0,30},{2,0},{4,2},{6,4},{8,6},{10,8},{12,10},{14,12},{16,14},{18,... | collective-permute-start | bytes 196616 | tf_op jit(solution)/shard_map/ppermute | solution.py:25
  219.6 6.4 %collective-permute-start.6 = (f32[64,256]{1,0:T(8,128)S(1)}, f32[64,256]{1,0:T(8,128)S(1)}, u32[]{:S(2)}, u32[]{:S(2)}) collective-permute-start(f32[64,256]{1,0:T(8,128)S(1)} %collective-permute-done.5), channel_id=1, source_target_pairs={{0,2},{2,4},{4,6},{6,8},{8,10},{10,12},{12,14},{14,16},{16,18},{18... | collective-permute-start | bytes 196616 | tf_op jit(solution)/shard_map/ppermute | solution.py:23
  219.6 6.4 %collective-permute-start.13 = (f32[64,256]{1,0:T(8,128)S(1)}, f32[64,256]{1,0:T(8,128)S(1)}, u32[]{:S(2)}, u32[]{:S(2)}) collective-permute-start(f32[64,256]{1,0:T(8,128)S(1)} %collective-permute-done.12), channel_id=1, source_target_pairs={{0,30},{2,0},{4,2},{6,4},{8,6},{10,8},{12,10},{14,12},{16,14},{18,... | collective-permute-start | bytes 196616 | tf_op jit(solution)/shard_map/ppermute | solution.py:25
  226.0 6.4 %collective-permute-start.7 = (f32[64,256]{1,0:T(8,128)S(1)}, f32[64,256]{1,0:T(8,128)S(1)}, u32[]{:S(2)}, u32[]{:S(2)}) collective-permute-start(f32[64,256]{1,0:T(8,128)S(1)} %collective-permute-done.6), channel_id=1, source_target_pairs={{0,2},{2,4},{4,6},{6,8},{8,10},{10,12},{12,14},{14,16},{16,18},{18... | collective-permute-start | bytes 196616 | tf_op jit(solution)/shard_map/ppermute | solution.py:23
  226.0 6.6 %collective-permute-start.14 = (f32[64,256]{1,0:T(8,128)S(1)}, f32[64,256]{1,0:T(8,128)S(1)}, u32[]{:S(2)}, u32[]{:S(2)}) collective-permute-start(f32[64,256]{1,0:T(8,128)S(1)} %collective-permute-done.13), channel_id=1, source_target_pairs={{0,30},{2,0},{4,2},{6,4},{8,6},{10,8},{12,10},{14,12},{16,14},{18,... | collective-permute-start | bytes 196616 | tf_op jit(solution)/shard_map/ppermute | solution.py:25
Sparse Core Ops, SparseCore 0:
  14.6 60.1 reduce-scatter.2
  77.2 36.8 all-gather.1
  123.8 56.3 reduce-scatter.4
